TPU v7x, 512 devices: a whole 4x4x16 slice. The times are simulated.
512 devices in a mesh: wa: 32 (over x, y, core), ha: 16 (over z).
Axes of the slice: x: 4, y: 4, z: 16, core: 2. Of those that a mesh axis runs over, the one named last changes fastest.
Arguments:
- residual_in: bfloat16 [192, 16384], P('ha', 'wa'), may hold values from -43.25 to 43.25
- grad_out: bfloat16 [192, 16384], P('ha', 'wa'), may hold values from -6 to 6
- norm_gain: bfloat16 [16384], P('wa'), may hold values from 0.099609375 to 1.8984375
- w_gate: bfloat16 [16384, 26624], P('wa', 'ha'), may hold values from -0.0390625 to 0.0390625
- w_up: bfloat16 [16384, 26624], P('wa', 'ha'), may hold values from -0.0390625 to 0.0390625
- w_down: bfloat16 [26624, 16384], P('ha', 'wa'), may hold values from -0.030643146 to 0.030643146
Outputs:
- grad_in: bfloat16 [192, 16384], P('ha', 'wa')
All inputs are finite; a program needn't handle non-finite values.
Results may differ from a plain program's by a relative error of at most 0.0053.
Values may be sent and summed in bfloat16 or wider, within the bound.
No kernel may reach another device: no remote copies, remote signals or barrier semaphores. Data moves between devices by JAX's collectives and lax.ppermute only.
A program may use at most 64 MiB of HBM per device.

v0:
```python
import jax
import jax.numpy as jnp
from jax import lax
from jax.sharding import Mesh
from jax.sharding import PartitionSpec as P

D = 16384
WA = ("x", "y", "core")


def gate_grads(gate, up, d_hidden):
    sig = jax.nn.sigmoid(gate)
    d_up = (d_hidden * gate * sig).astype(jnp.bfloat16)
    d_gate = (d_hidden * up * sig * (1.0 + gate * (1.0 - sig))).astype(jnp.bfloat16)
    return (d_gate, d_up)


def local(residual_in, grad_out, norm_gain, w_gate, w_up, w_down):
    rows = residual_in.shape[0]
    gain_f = norm_gain.astype(jnp.float32)
    piece = lax.all_gather(jnp.stack([residual_in, grad_out]), "ha", axis=1, tiled=True)
    stream_all = piece[0].astype(jnp.float32)
    squares = jnp.sum(stream_all * stream_all, axis=1)
    squares = lax.psum(lax.psum(lax.psum(squares, "core"), "y"), "x")
    inv_rms_all = lax.rsqrt(squares / D + 1e-05)[:, None]
    normed = (stream_all * inv_rms_all * gain_f).astype(jnp.bfloat16)
    gate_part = jnp.dot(normed, w_gate, preferred_element_type=jnp.float32)
    up_part = jnp.dot(normed, w_up, preferred_element_type=jnp.float32)
    back_part = lax.dot_general(
        piece[1], w_down, (((1,), (1,)), ((), ())), preferred_element_type=jnp.float32
    )
    summed = lax.psum(jnp.stack([gate_part, up_part, back_part]), WA)
    gate, up, d_hidden = (summed[0], summed[1], summed[2])
    d_gate, d_up = gate_grads(gate, up, d_hidden)
    dot_part = jnp.sum(d_gate.astype(jnp.float32) * gate + d_up.astype(jnp.float32) * up, axis=1)
    total = lax.dot_general(
        d_gate, w_gate, (((1,), (1,)), ((), ())), preferred_element_type=jnp.float32
    ) + lax.dot_general(d_up, w_up, (((1,), (1,)), ((), ())), preferred_element_type=jnp.float32)
    n_ha, width = (lax.axis_size("ha"), total.shape[1])
    dot_rows = jnp.pad(dot_part.reshape(n_ha, 1, rows), ((0, 0), (0, 0), (0, width - rows)))
    packed = jnp.concatenate([total.reshape(n_ha, rows, width), dot_rows], axis=1)
    mine = lax.psum_scatter(packed.reshape(-1, width), "ha", scatter_dimension=0, tiled=True)
    d_normed = mine[:rows]
    start = lax.axis_index("ha") * rows
    inv_rms = lax.dynamic_slice_in_dim(inv_rms_all, start, rows, axis=0)
    row_dot = mine[rows, :rows][:, None] / inv_rms
    stream = residual_in.astype(jnp.float32)
    scaled = d_normed * gain_f
    grad_in = grad_out.astype(jnp.float32) + inv_rms * scaled - stream * inv_rms**3 * row_dot / D
    return grad_in.astype(jnp.bfloat16)


def solution(mesh):
    devices = mesh.devices if mesh.axis_names[0] == "wa" else mesh.devices.T
    view = Mesh(devices.reshape(4, 4, 2, devices.shape[1]), WA + ("ha",))
    placed = (P("ha", WA), P("ha", WA), P(WA), P(WA, "ha"), P(WA, "ha"), P("ha", WA))
    return jax.shard_map(local, mesh=view, in_specs=placed, out_specs=P("ha", WA), check_vma=False)
```

profile of v0, /device:TPU:2, one launch (start us, length us, event | category | flops | bytes accessed | tf_op | source)
XLA Modules:
  0.0 363.5 jit_solution(15139991436451758172)
XLA Ops:
  6.5 0.9 pad_maximum_fusion.1
  7.5 37.8 %all_gather.3 = bf16[2,192,512]{2,0,1:T(2,128)(2,1)S(1)} all-gather(bf16[2,12,512]{2,0,1:T(2,128)(2,1)S(1)} %copy.9), channel_id=1, replica_groups=mesh['x'=4,'y'=4,'core'=2,'ha'=16] {'ha'}, dimensions={1}, use_global_device_ids=true | all-gather | bytes 417792 | tf_op jit(solution)/shard_map/all_gather | solution.py:21
  45.3 1.3 slice_convert_fusion
  46.6 0.7 copy-done.2
  47.3 0.1 fusion
  47.4 2.5 psum.28
  49.9 10.7 %psum.29 = f32[192]{0:T(256)S(1)} all-reduce(f32[192]{0:T(256)S(1)} %psum.28), channel_id=1, replica_groups=mesh['x'=4,'y'=4,'core'=2,'ha'=16] {'y'}, use_global_device_ids=true, to_apply=%region_2.0 | all-reduce | flops 192 | bytes 1536 | tf_op jit(solution)/shard_map/psum | solution.py:24
  60.6 8.6 %psum.30 = f32[192]{0:T(256)S(1)} all-reduce(f32[192]{0:T(256)S(1)} %psum.29), channel_id=1, replica_groups=mesh['x'=4,'y'=4,'core'=2,'ha'=16] {'x'}, use_global_device_ids=true, to_apply=%region_3.0 | all-reduce | flops 192 | bytes 1536 | tf_op jit(solution)/shard_map/psum | solution.py:24
  69.3 1.6 convolution_bitcast_fusion.1
  70.9 0.6 convolution_bitcast_fusion.2
  71.5 0.8 copy-done.4
  72.4 0.7 convolution_bitcast_fusion
  73.2 2.1 pad_maximum_fusion
  75.4 134.0 %all-reduce.5.cloned.1.call-done = f32[3,192,1664]{2,1,0:T(8,128)} async-done(((f32[3,192,1664]{2,1,0:T(8,128)}), f32[3,192,1664]{2,1,0:T(8,128)}) %all-reduce.5.cloned.1.call-update) | async-done | bytes 3833872 | tf_op jit(solution)/shard_map/psum | solution.py:32
  209.3 2.9 add_reduce_fusion
  212.3 0.7 fusion.11
  213.0 1.5 convolution_add_fusion
  214.5 1.0 reshape.21
  215.7 0.8 reshape.23
  216.5 1.3 dynamic-slice.4
  218.4 0.1 multiply_multiply_fusion
  218.5 136.0 %all-reduce.7.cloned.1.call-done = f32[208,512]{1,0:T(8,128)} async-done(((f32[208,512]{1,0:T(8,128)}), f32[208,512]{1,0:T(8,128)}) %all-reduce.7.cloned.1.call-update) | async-done | bytes 426000
  354.5 0.7 fusion.8
  355.2 1.5 fusion.6
  (25 shorter events, 0.3 us)
Async XLA Ops:
  6.5 64.4 %copy-start = (bf16[512,1664]{1,0:T(8,128)(2,1)S(1)}, bf16[512,1664]{1,0:T(8,128)(2,1)}, u32[]{:S(2)}) copy-start(bf16[512,1664]{1,0:T(8,128)(2,1)} %param.9) | copy-start | bytes 5111812
  6.5 62.7 %copy-start.8 = (bf16[512]{0:T(512)(128)(2,1)S(1)}, bf16[512]{0:T(512)(128)(2,1)}, u32[]{:S(2)}) copy-start(bf16[512]{0:T(512)(128)(2,1)} %param.8) | copy-start | bytes 3076
  6.5 62.7 %copy-start.1 = (bf16[512,1664]{1,0:T(8,128)(2,1)S(1)}, bf16[512,1664]{1,0:T(8,128)(2,1)}, u32[]{:S(2)}) copy-start(bf16[512,1664]{1,0:T(8,128)(2,1)} %param.10) | copy-start | bytes 5111812
  6.5 202.8 %all-reduce.5.cloned.1.call-start = ((), (), s32[]{:S(2)}) async-start(), calls=%async_computation | async-start | bytes 7667712 | tf_op jit(solution)/shard_map/psum | solution.py:32
  46.6 0.7 copy-start.2
  69.2 1.7 copy-start.3
  70.9 1.5 copy-start.4
  70.9 1.5 copy-start.5
  75.3 279.2 %all-reduce.7.cloned.1.call-start = ((), (), s32[]{:S(2)}) async-start(), calls=%async_computation.1 | async-start | bytes 851968
  215.5 139.7 %copy-start.6 = (bf16[12,512]{1,0:T(8,128)(2,1)S(1)}, bf16[12,512]{1,0:T(8,128)(2,1)}, u32[]{:S(2)}) copy-start(bf16[12,512]{1,0:T(8,128)(2,1)} %param.7) | copy-start | bytes 36868
  215.5 139.7 %copy-start.7 = (bf16[12,512]{1,0:T(8,128)(2,1)S(1)}, bf16[12,512]{1,0:T(8,128)(2,1)}, u32[]{:S(2)}) copy-start(bf16[12,512]{1,0:T(8,128)(2,1)} %param.6) | copy-start | bytes 36868
Sparse Core Ops, SparseCore 0:
  75.4 133.8 all-reduce.4
  216.6 137.8 all-reduce.6
where the time goes:
time: 364 us
  waiting for transfers between devices  270 us (74%)
  blocking collectives  59.6 us (16%)
  between operations  14.2 us (4%)
  other arithmetic  9.68 us (3%)
  matrix products  5.11 us (1%)
  local copies, waits for them, and re-layouts  4.91 us (1%)
    unnamed x3, waiting for transfers between devices  136 us
    psum x1, waiting for transfers between devices, local(): summed = lax.psum(jnp.stack([gate_part, up_part, back_part]), WA)  134 us
    all_gather x1, blocking collectives, local(): lax.all_gather(jnp.stack([residual_in, grad_out]), 'ha', axis=1, tiled=True)  37.8 us
    psum x3, blocking collectives, local(): squares = lax.psum(lax.psum(lax.psum(squares, 'core'), 'y'), 'x')  21.8 us
  transfers between devices with their start and end apart: 2, of which 2 were waited for; matrix products, arithmetic and copies ran while one was open for 0% of the time, Pallas kernels for 0%

commit v1 on v0

--- a/solution.py
+++ b/solution.py
@@ -1,11 +1,22 @@
+import functools
 import jax
 import jax.numpy as jnp
 from jax import lax
 from jax.sharding import Mesh
 from jax.sharding import PartitionSpec as P
+from jax.lax import all_to_all, axis_size
 
 D = 16384
 WA = ("x", "y", "core")
+
+
+def name_signs(incoming_x, link_axis, pos_dim):
+    later = jnp.stack(axis_size(link_axis) * [incoming_x])
+    response = all_to_all(later, link_axis, 0, 0)
+    return jnp.concatenate(response, pos_dim)
+
+
+push_joints = functools.partial(name_signs, link_axis="ha", pos_dim=1)
 
 
 def gate_grads(gate, up, d_hidden):
@@ -18,7 +29,7 @@
 def local(residual_in, grad_out, norm_gain, w_gate, w_up, w_down):
     rows = residual_in.shape[0]
     gain_f = norm_gain.astype(jnp.float32)
-    piece = lax.all_gather(jnp.stack([residual_in, grad_out]), "ha", axis=1, tiled=True)
+    piece = push_joints(jnp.stack([residual_in, grad_out]))
     stream_all = piece[0].astype(jnp.float32)
     squares = jnp.sum(stream_all * stream_all, axis=1)
     squares = lax.psum(lax.psum(lax.psum(squares, "core"), "y"), "x")

time: 364 us -> 376 us (1.033)
  blocking collectives: 59.6 us -> 21.8 us
  waiting for transfers between devices: 270 us -> 293 us
  starting transfers between devices: 0.04 us -> 15.3 us
  local copies, waits for them, and re-layouts: 4.91 us -> 10.7 us
  matrix products: 5.11 us -> 8.93 us
    all_gather x1 -> x0, blocking collectives: 37.8 us -> none  [local(): lax.all_gather(jnp.stack([residual_in, grad_out]), 'ha', axis=1, tiled=True)]
    all_to_all x0 -> x1, waiting for transfers between devices: none -> 23.8 us  [name_signs(): response = all_to_all(later, link_axis, 0, 0)]
    all_to_all x0 -> x1, starting transfers between devices: none -> 15.2 us  [name_signs(): response = all_to_all(later, link_axis, 0, 0)]
  transfers between devices with their start and end apart: 2 -> 3, of which waited for: 2 -> 3; matrix products, arithmetic and copies ran while one was open for 0% -> 0% of each run, Pallas kernels for 0% -> 0%
where the time goes in v1:
time: 376 us
  waiting for transfers between devices  293 us (78%)
  blocking collectives  21.8 us (6%)
  starting transfers between devices  15.3 us (4%)
  between operations  14.2 us (4%)
  other arithmetic  11.7 us (3%)
  local copies, waits for them, and re-layouts  10.7 us (3%)
  matrix products  8.93 us (2%)
    unnamed x3, waiting for transfers between devices  136 us
    psum x1, waiting for transfers between devices, local(): summed = lax.psum(jnp.stack([gate_part, up_part, back_part]), WA)  133 us
    all_to_all x1, waiting for transfers between devices, name_signs(): response = all_to_all(later, link_axis, 0, 0)  23.8 us
    psum x3, blocking collectives, local(): squares = lax.psum(lax.psum(lax.psum(squares, 'core'), 'y'), 'x')  21.8 us
    all_to_all x1, starting transfers between devices, name_signs(): response = all_to_all(later, link_axis, 0, 0)  15.2 us
  transfers between devices with their start and end apart: 3, of which 3 were waited for; matrix products, arithmetic and copies ran while one was open for 0% of the time, Pallas kernels for 0%

profile of v1, /device:TPU:2, one launch (start us, length us, event | category | flops | bytes accessed | tf_op | source)
XLA Modules:
  0.0 375.6 jit_solution(295224722900182479)
XLA Ops:
  6.5 0.9 pad_maximum_fusion.1
  7.5 0.9 stack.19
  8.4 15.2 %all-to-all-start = ((bf16[16,2,12,512]{3,1,2,0:T(2,128)(2,1)}), bf16[16,2,12,512]{3,1,2,0:T(2,128)(2,1)}, u32[]{:S(2)}, u32[]{:S(2)}) async-start(bf16[16,2,12,512]{3,1,2,0:T(2,128)(2,1)} %stack.19), calls=%async_computation | async-start | bytes 786432 | tf_op jit(solution)/shard_map/all_to_all | solution.py:15
  23.7 23.8 %all-to-all-done = bf16[16,2,12,512]{3,1,2,0:T(2,128)(2,1)} async-done(((bf16[16,2,12,512]{3,1,2,0:T(2,128)(2,1)}), bf16[16,2,12,512]{3,1,2,0:T(2,128)(2,1)}, u32[]{:S(2)}, u32[]{:S(2)}) %all-to-all-start) | async-done | bytes 393248 | tf_op jit(solution)/shard_map/all_to_all | solution.py:15
  47.5 3.4 multiply_reduce_fusion
  50.9 2.9 slice_reduce_fusion
  53.9 2.5 psum.28
  56.3 10.7 %psum.29 = f32[192]{0:T(256)S(1)} all-reduce(f32[192]{0:T(256)S(1)} %psum.28), channel_id=1, replica_groups=mesh['x'=4,'y'=4,'core'=2,'ha'=16] {'y'}, use_global_device_ids=true, to_apply=%region_2.0 | all-reduce | flops 192 | bytes 1536 | tf_op jit(solution)/shard_map/psum | solution.py:35
  67.0 8.6 %psum.30 = f32[192]{0:T(256)S(1)} all-reduce(f32[192]{0:T(256)S(1)} %psum.29), channel_id=1, replica_groups=mesh['x'=4,'y'=4,'core'=2,'ha'=16] {'x'}, use_global_device_ids=true, to_apply=%region_3.0 | all-reduce | flops 192 | bytes 1536 | tf_op jit(solution)/shard_map/psum | solution.py:35
  75.7 1.8 reshape.36
  77.5 2.7 convolution_bitcast_fusion.1
  80.2 1.6 convolution_bitcast_fusion.2
  81.9 1.7 squeeze.13
  83.5 2.4 convolution_bitcast_fusion
  86.0 2.1 pad_maximum_fusion
  88.2 133.3 %all-reduce.5.cloned.1.call-done = f32[3,192,1664]{2,1,0:T(8,128)} async-done(((f32[3,192,1664]{2,1,0:T(8,128)}), f32[3,192,1664]{2,1,0:T(8,128)}) %all-reduce.5.cloned.1.call-update) | async-done | bytes 3833872 | tf_op jit(solution)/shard_map/psum | solution.py:43
  221.5 2.9 add_reduce_fusion
  224.4 0.7 fusion.7
  225.1 1.5 convolution_add_fusion
  226.6 1.0 reshape.33
  227.8 0.8 reshape.35
  228.6 1.3 dynamic-slice.4
  230.6 136.0 %all-reduce.7.cloned.1.call-done = f32[208,512]{1,0:T(8,128)} async-done(((f32[208,512]{1,0:T(8,128)}), f32[208,512]{1,0:T(8,128)}) %all-reduce.7.cloned.1.call-update) | async-done | bytes 426000
  367.3 1.5 fusion.4
  (28 shorter events, 1.2 us)
Async XLA Ops:
  6.5 73.7 %copy-start = (bf16[512,1664]{1,0:T(8,128)(2,1)S(1)}, bf16[512,1664]{1,0:T(8,128)(2,1)}, u32[]{:S(2)}) copy-start(bf16[512,1664]{1,0:T(8,128)(2,1)} %param.9) | copy-start | bytes 5111812
  6.5 17.2 %copy-start.7 = (bf16[512]{0:T(512)(128)(2,1)S(1)}, bf16[512]{0:T(512)(128)(2,1)}, u32[]{:S(2)}) copy-start(bf16[512]{0:T(512)(128)(2,1)} %param.8) | copy-start | bytes 3076
  8.4 39.1 %all-to-all-start = ((bf16[16,2,12,512]{3,1,2,0:T(2,128)(2,1)}), bf16[16,2,12,512]{3,1,2,0:T(2,128)(2,1)}, u32[]{:S(2)}, u32[]{:S(2)}) async-start(bf16[16,2,12,512]{3,1,2,0:T(2,128)(2,1)} %stack.19), calls=%async_computation | async-start | bytes 786432 | tf_op jit(solution)/shard_map/all_to_all | solution.py:15
  23.6 53.9 %copy-start.1 = (bf16[512,1664]{1,0:T(8,128)(2,1)S(1)}, bf16[512,1664]{1,0:T(8,128)(2,1)}, u32[]{:S(2)}) copy-start(bf16[512,1664]{1,0:T(8,128)(2,1)} %param.10) | copy-start | bytes 5111812
  23.7 197.8 %all-reduce.5.cloned.1.call-start = ((), (), s32[]{:S(2)}) async-start(), calls=%async_computation.1 | async-start | bytes 7667712 | tf_op jit(solution)/shard_map/psum | solution.py:43
  77.5 2.7 copy-start.4
  83.5 2.4 copy-start.2
  83.5 2.4 copy-start.3
  88.1 278.5 %all-reduce.7.cloned.1.call-start = ((), (), s32[]{:S(2)}) async-start(), calls=%async_computation.2 | async-start | bytes 851968
  227.6 139.7 %copy-start.5 = (bf16[12,512]{1,0:T(8,128)(2,1)S(1)}, bf16[12,512]{1,0:T(8,128)(2,1)}, u32[]{:S(2)}) copy-start(bf16[12,512]{1,0:T(8,128)(2,1)} %param.7) | copy-start | bytes 36868
  227.6 139.7 %copy-start.6 = (bf16[12,512]{1,0:T(8,128)(2,1)S(1)}, bf16[12,512]{1,0:T(8,128)(2,1)}, u32[]{:S(2)}) copy-start(bf16[12,512]{1,0:T(8,128)(2,1)} %param.6) | copy-start | bytes 36868
Sparse Core Ops, SparseCore 0:
  88.2 133.1 all-reduce.4
  228.7 137.8 all-reduce.6
